TPU v7x, 128 devices: a whole 4x4x4 slice. The times are simulated.
128 devices in a mesh: seq: 16 (over y, x), grp: 8 (over z, core).
Axes of the slice: x: 4, y: 4, z: 4, core: 2. Of those that a mesh axis runs over, the one named last changes fastest.
Arguments:
- patches: bfloat16 [16384, 1664], P(('grp', 'seq')), may hold values from -6 to 6
- vis_gain: float32 [1664], replicated, may hold values from 0.25 to 1.75
- vis_qkv: bfloat16 [3, 1664, 1664], P(None, None, 'seq')
- vis_out: bfloat16 [1664, 1664], P('seq'), may hold values from -0.15625 to 0.15625
- merge_gain: float32 [1664], replicated, may hold values from 0.25 to 1.75
- merge_w: bfloat16 [6656, 1664], P('seq'), may hold values from -0.078125 to 0.078125
- image_blocks: int32 [8, 4], P('grp'), may hold values from 1 to 256, 512 in all within a row
- dest_group: int32 [4096, 1], P(('grp', 'seq')), may hold values from 0 to 7; in each aligned block of 32 rows (0 to 31, 32 to 63, ...) at most 8 rows name the same one
- slot_rows: int32 [8, 16, 128], P('grp', 'seq'), may hold values from 0 to 127, each once within a row
- prompt_len: int32 [8], P('grp'), may hold values from 512 to 2048
- text_emb: bfloat16 [16384, 1664], P(('grp', 'seq')), may hold values from -6 to 6
- txt_gain: float32 [1664], replicated, may hold values from 0.25 to 1.75
- txt_qkv: bfloat16 [3, 1664, 1664], P(None, None, 'seq')
- txt_out: bfloat16 [1664, 1664], P('seq'), may hold values from -0.15625 to 0.15625
Outputs:
- text_out: float32 [16384, 1664], P(('grp', 'seq'))
Inputs may be any that keep to these rules, and one draw needn't show every extreme that they name: image_blocks[g] sum to 512; one image of every group has the most. `dest_group`: of the 32 merged tokens of one device (aligned blocks of rows), at most 8 name one group. slot_rows[q, s] is a permutation of 0 to 127.
All inputs are finite; a program needn't handle non-finite values.
Results may differ from a plain program's by a relative error of at most 0.012.
Values may be sent and summed in bfloat16 or wider, within the bound.
No kernel may reach another device: no remote copies, remote signals or barrier semaphores. Data moves between devices by JAX's collectives and lax.ppermute only.
A program may use at most 64 MiB of HBM per device.

v0:
```python
import jax
import jax.numpy as jnp
from jax import lax
from jax.sharding import PartitionSpec as P

HEAD_DIM = 104


def layer_norm(row_block, scale_gain):
    values_f = row_block.astype(jnp.float32)
    row_mean = jnp.mean(values_f, axis=-1, keepdims=True)
    centred = values_f - row_mean
    variance = jnp.mean(centred * centred, axis=-1, keepdims=True)
    return centred * lax.rsqrt(variance + 1e-06) * scale_gain


def rms_norm(row_block, scale_gain):
    values_f = row_block.astype(jnp.float32)
    return (
        values_f
        * lax.rsqrt(jnp.mean(values_f * values_f, axis=-1, keepdims=True) + 1e-06)
        * scale_gain
    )


def projector(weights, shard_piece):
    count, width, head_width = weights.shape
    packed = weights.transpose(1, 0, 2).reshape(width, count * head_width)
    joined = jnp.dot(shard_piece, packed, preferred_element_type=jnp.float32).astype(jnp.bfloat16)
    return joined.reshape(shard_piece.shape[0], count, head_width).transpose(1, 0, 2)


def attend_local(queries, key_rows, value_rows, allowed_fn):
    length = queries.shape[0]
    head_width = queries.shape[1]
    head_count = head_width // HEAD_DIM
    block_rows = min(512, length)
    block_count = length // block_rows
    query_blocks = queries.reshape(block_count, block_rows, head_count, HEAD_DIM)
    key_heads = key_rows.reshape(length, head_count, HEAD_DIM)
    value_heads = value_rows.reshape(length, head_count, HEAD_DIM)

    def one_block(block_item):
        query_part, first_row = block_item
        scores = jnp.einsum(
            "qhe,khe->hqk", query_part, key_heads, preferred_element_type=jnp.float32
        ) * HEAD_DIM ** (-0.5)
        allowed = allowed_fn(first_row + jnp.arange(block_rows, dtype=jnp.int32))
        scores = jnp.where(allowed[None], scores, -1e30)
        row_max = jnp.max(scores, axis=-1, keepdims=True)
        expo = jnp.exp(scores - row_max)
        probabilities = (expo / jnp.sum(expo, axis=-1, keepdims=True)).astype(jnp.bfloat16)
        return jnp.einsum(
            "hqk,khe->qhe", probabilities, value_heads, preferred_element_type=jnp.float32
        ).astype(jnp.bfloat16)

    starts = jnp.arange(block_count, dtype=jnp.int32) * block_rows
    joined = lax.map(one_block, (query_blocks, starts))
    return joined.reshape(length, head_width)


def heads_to_rows(heads, seq_count):
    length, width = heads.shape
    rows = length // seq_count
    blocks = heads.reshape(seq_count, rows, width)
    swapped = lax.all_to_all(blocks, "seq", split_axis=0, concat_axis=0, tiled=True)
    return swapped.transpose(1, 0, 2).reshape(rows, seq_count * width)


def attend_causal(queries, key_rows, value_rows, allowed_fn):
    length = queries.shape[0]
    head_width = queries.shape[1]
    head_count = head_width // HEAD_DIM
    block_rows = min(512, length)
    block_count = length // block_rows
    key_heads = key_rows.reshape(length, head_count, HEAD_DIM)
    value_heads = value_rows.reshape(length, head_count, HEAD_DIM)
    outputs = []
    for block in range(block_count):
        first_row = block * block_rows
        key_end = first_row + block_rows
        query_part = queries[first_row:key_end].reshape(block_rows, head_count, HEAD_DIM)
        scores = jnp.einsum(
            "qhe,khe->hqk", query_part, key_heads[:key_end], preferred_element_type=jnp.float32
        ) * HEAD_DIM ** (-0.5)
        allowed = allowed_fn(first_row + jnp.arange(block_rows, dtype=jnp.int32))[:, :key_end]
        scores = jnp.where(allowed[None], scores, -1e30)
        row_max = jnp.max(scores, axis=-1, keepdims=True)
        expo = jnp.exp(scores - row_max)
        probabilities = (expo / jnp.sum(expo, axis=-1, keepdims=True)).astype(jnp.bfloat16)
        outputs.append(
            jnp.einsum(
                "hqk,khe->qhe",
                probabilities,
                value_heads[:key_end],
                preferred_element_type=jnp.float32,
            ).astype(jnp.bfloat16)
        )
    return jnp.concatenate(outputs, axis=0).reshape(length, head_width)


def per_device(
    patches,
    vis_gain,
    vis_qkv,
    vis_out,
    merge_gain,
    merge_w,
    image_blocks,
    dest_group,
    slot_rows,
    prompt_len,
    text_emb,
    txt_gain,
    txt_qkv,
    txt_out,
):
    seq_count = lax.axis_size("seq")
    groups = lax.axis_size("grp")
    token_count = patches.shape[0]
    model_width = patches.shape[1]
    group_patches = token_count * seq_count
    vis_out_full = lax.all_gather(vis_out, "seq", axis=0, tiled=True)
    vis_normed = layer_norm(patches, vis_gain).astype(jnp.bfloat16)
    vis_proj = projector(vis_qkv, lax.all_gather(vis_normed, "seq", axis=0, tiled=True))
    bounds = jnp.cumsum(image_blocks[0])[:-1]

    def segment(indices):
        return jnp.sum(((indices // 4)[:, None] >= bounds[None, :]).astype(jnp.int32), axis=1)

    key_segments = segment(jnp.arange(group_patches, dtype=jnp.int32))

    def vis_allowed(row_indices):
        return segment(row_indices)[:, None] == key_segments[None, :]

    vis_heads = attend_local(vis_proj[0], vis_proj[1], vis_proj[2], vis_allowed)
    vis_heads, txt_out = lax.optimization_barrier((vis_heads, txt_out))
    txt_out_full = lax.all_gather(txt_out, "seq", axis=0, tiled=True)
    vis_attn = jnp.dot(
        heads_to_rows(vis_heads, seq_count), vis_out_full, preferred_element_type=jnp.float32
    )
    residual_sum = patches.astype(jnp.float32) + vis_attn
    merged_in = (
        layer_norm(residual_sum, merge_gain)
        .astype(jnp.bfloat16)
        .reshape(token_count // 4, 4 * model_width)
    )
    feature_slices = lax.all_to_all(merged_in, "seq", split_axis=1, concat_axis=0, tiled=True)
    merge_partial = jnp.dot(feature_slices, merge_w, preferred_element_type=jnp.float32)
    merge_parts = lax.all_to_all(
        merge_partial.astype(jnp.bfloat16).reshape(seq_count, -1, model_width),
        "seq",
        split_axis=0,
        concat_axis=0,
        tiled=True,
    )
    visual = jnp.sum(merge_parts.astype(jnp.float32), axis=0).astype(jnp.bfloat16)
    dest_rows = dest_group[:, 0]
    merged_rows = dest_rows.shape[0]
    capacity = max(2, 2 * merged_rows // groups)
    onehot = (dest_rows[:, None] == jnp.arange(groups, dtype=jnp.int32)[None, :]).astype(jnp.int32)
    slot_rank = jnp.sum((jnp.cumsum(onehot, axis=0) - 1) * onehot, axis=1)
    selector = (
        (dest_rows[None, None, :] == jnp.arange(groups, dtype=jnp.int32)[:, None, None])
        & (slot_rank[None, None, :] == jnp.arange(capacity, dtype=jnp.int32)[None, :, None])
    ).astype(jnp.bfloat16)
    outgoing = jnp.einsum(
        "gct,td->gcd", selector, visual, preferred_element_type=jnp.float32
    ).astype(jnp.bfloat16)
    arrived_flags = jnp.sum(selector.astype(jnp.float32), axis=2).astype(jnp.bfloat16)
    flag_row = jnp.pad(arrived_flags, ((0, 0), (0, model_width - capacity)))[:, None, :]
    payload = lax.all_to_all(
        jnp.concatenate([outgoing, flag_row], axis=1),
        "grp",
        split_axis=0,
        concat_axis=0,
        tiled=True,
    )
    incoming = payload[:, :capacity, :]
    arrived = payload[:, capacity, :capacity]
    prompt_rows = text_emb.shape[0]
    slot_targets = slot_rows[0, 0, : groups * capacity]
    placement_map = (
        slot_targets[None, :] == jnp.arange(prompt_rows, dtype=jnp.int32)[:, None]
    ).astype(jnp.bfloat16)
    placement_map = placement_map * arrived.reshape(1, groups * capacity)
    replaced = jnp.sum(placement_map.astype(jnp.float32), axis=1, keepdims=True)
    placed = jnp.dot(
        placement_map,
        incoming.reshape(groups * capacity, model_width),
        preferred_element_type=jnp.float32,
    )
    hidden = (text_emb.astype(jnp.float32) * (1.0 - replaced) + placed).astype(jnp.bfloat16)
    txt_normed = rms_norm(hidden, txt_gain).astype(jnp.bfloat16)
    txt_normed, txt_out_full = lax.optimization_barrier((txt_normed, txt_out_full))
    txt_proj = projector(txt_qkv, lax.all_gather(txt_normed, "seq", axis=0, tiled=True))
    length = prompt_len[0]
    key_positions = jnp.arange(prompt_rows * seq_count, dtype=jnp.int32)

    def txt_allowed(row_indices):
        return (key_positions[None, :] <= row_indices[:, None]) & (key_positions[None, :] < length)

    txt_heads = attend_causal(txt_proj[0], txt_proj[1], txt_proj[2], txt_allowed)
    txt_attn = jnp.dot(
        heads_to_rows(txt_heads, seq_count), txt_out_full, preferred_element_type=jnp.float32
    )
    return hidden.astype(jnp.float32) + txt_attn


def solution(mesh):
    in_specs = (
        P(("grp", "seq"), None),
        P(),
        P(None, None, "seq"),
        P("seq", None),
        P(),
        P("seq", None),
        P("grp", None),
        P(("grp", "seq"), None),
        P("grp", "seq", None),
        P("grp"),
        P(("grp", "seq"), None),
        P(),
        P(None, None, "seq"),
        P("seq", None),
    )
    out_specs = P(("grp", "seq"), None)
    return jax.shard_map(
        per_device, mesh=mesh, in_specs=in_specs, out_specs=out_specs, check_vma=False
    )
```

profile of v0, /device:TPU:0, one launch (start us, length us, event | category | flops | bytes accessed | tf_op | source)
XLA Modules:
  0.0 321.0 jit_solution(7446433832728544742)
XLA Ops:
  6.5 1.3 convert_reduce_fusion.1
  7.8 1.3 fusion.35
  9.1 2.1 fusion.37
  11.2 0.7 all-gather.7.cloned.1.call-update
  12.0 0.8 reduce-window.4
  12.9 64.4 %all-gather.5.cloned.1.call-done = bf16[2048,1664]{1,0:T(8,128)(2,1)} async-done(((bf16[128,1664]{1,0:T(8,128)(2,1)}), bf16[2048,1664]{1,0:T(8,128)(2,1)}) %all-gather.5.cloned.1.call-update) | async-done | bytes 6815760 | tf_op jit(solution)/shard_map/all_gather | solution.py:125
  77.4 5.7 %convolution_convert_fusion.2 = bf16[2048,312]{0,1:T(8,128)(2,1)S(1)} fusion(bf16[2048,1664]{1,0:T(8,128)(2,1)} %all-gather.5.cloned.1.call-done, bf16[1664,312]{0,1:T(8,128)(2,1)} %bitcast.189), kind=kOutput, calls=%fused_computation.38 | convolution fusion | flops 2127151104 | bytes 9132032 | tf_op jit(solution)/shard_map/dot_general | solution.py:29
  83.6 16.5 %while.12 = (s32[]{:T(128)}, bf16[4,512,1,104]{1,3,2,0:T(8,128)(2,1)S(1)}, s32[4]{0:T(128)S(1)}, s32[3]{0:T(128)S(1)}, s32[2048]{0:T(1024)S(1)}, /*index=5*/bf16...) while((s32[]{:T(128)}, ...), condition=%wide.region_10.11_spmd, body=%wide.region_6.10_spmd.sunk | while | flops 445709312 | bytes 13674625 | solution.py:58
  84.2 0.7 add_select_fusion.3
  84.9 1.0 fusion.75
  85.9 0.7 fusion.76
  86.6 1.1 fusion.77
  88.3 0.7 add_select_fusion.3
  89.1 1.0 fusion.75
  90.0 0.7 fusion.76
  90.8 1.1 fusion.77
  92.4 0.7 add_select_fusion.3
  93.2 1.0 fusion.75
  94.2 0.7 fusion.76
  94.9 1.1 fusion.77
  97.3 1.0 fusion.75
  98.3 0.7 fusion.76
  99.0 1.1 fusion.77
  100.5 0.8 copy_bitcast_fusion
  101.3 5.3 %all-to-all-start = ((bf16[16,128,104]{1,2,0:T(8,128)(2,1)}), bf16[16,128,104]{1,2,0:T(8,128)(2,1)S(1)}, u32[]{:S(2)}, u32[]{:S(2)}) async-start(bf16[16,128,104]{1,2,0:T(8,128)(2,1)} %copy_bitcast_fusion), calls=%async_computation | async-start | bytes 851968 | tf_op jit(solution)/shard_map/all_to_all | solution.py:66
  106.6 31.9 %all-gather.7.cloned.1.call-done = bf16[1664,1664]{1,0:T(8,128)(2,1)} async-done(((bf16[104,1664]{1,0:T(8,128)(2,1)}), bf16[1664,1664]{1,0:T(8,128)(2,1)}) %all-gather.7.cloned.1.call-update) | async-done | bytes 5537808 | tf_op jit(solution)/shard_map/all_gather | solution.py:123
  138.5 3.7 %fusion.54 = (f32[128]{0:T(128)S(1)}, f32[128,1664]{1,0:T(8,128)S(1)}) fusion(bf16[128,1664]{0,1:T(8,128)(2,1)S(1)} %bitcast.177, bf16[1664,1664]{1,0:T(8,128)(2,1)} %all-gather.7.cloned.1.call-done, bf16[128,1664]{1,0:T(8,128)(2,1)S(1)} %copy-done.1), kind=kOutput, calls=%fused_computation.139 | convolution fusion | flops 709476224 | bytes 7242240 | tf_op jit(solution)/shard_map/dot_general | solution.py:139
  143.6 19.0 %all_to_all.39 = bf16[32,16,416]{2,0,1:T(8,128)(2,1)S(1)} all-to-all(bf16[32,16,416]{2,0,1:T(8,128)(2,1)S(1)} %copy.31), channel_id=1, replica_groups=mesh['seq'=16,'grp'=8] {'seq'}, dimensions={1} | all-to-all | bytes 851968 | tf_op jit(solution)/shard_map/all_to_all | solution.py:148
  162.6 2.3 convolution_convert_fusion
  164.9 3.8 %all-to-all-start.2 = ((bf16[16,32,1664]{2,1,0:T(8,128)(2,1)}), bf16[16,32,1664]{2,1,0:T(8,128)(2,1)S(1)}, u32[]{:S(2)}, u32[]{:S(2)}) async-start(bf16[16,32,1664]{2,1,0:T(8,128)(2,1)} %bitcast.178), calls=%async_computation.2 | async-start | bytes 3407872 | tf_op jit(solution)/shard_map/all_to_all | solution.py:150
  168.9 0.9 select_reduce_fusion
  169.8 0.7 iota_compare_fusion.5
  170.5 0.7 copy.32
  171.2 34.2 %all-to-all-done.2 = bf16[16,32,1664]{2,1,0:T(8,128)(2,1)S(1)} async-done(((bf16[16,32,1664]{2,1,0:T(8,128)(2,1)}), bf16[16,32,1664]{2,1,0:T(8,128)(2,1)S(1)}, u32[]{:S(2)}, u32[]{:S(2)}) %all-to-all-start.2) | async-done | bytes 1703968 | tf_op jit(solution)/shard_map/all_to_all | solution.py:150
  205.4 0.9 reduce_sum.159
  206.3 1.1 convolution_convert_fusion.3
  207.4 1.6 pad_maximum_fusion
  209.0 4.5 %all-to-all-start.3 = ((bf16[8,9,1664]{2,1,0:T(8,128)(2,1)}), bf16[8,9,1664]{2,1,0:T(8,128)(2,1)S(1)}, u32[]{:S(2)}, u32[]{:S(2)}) async-start(bf16[8,9,1664]{2,1,0:T(8,128)(2,1)} %pad_maximum_fusion), calls=%async_computation.3 | async-start | bytes 851968 | tf_op jit(solution)/shard_map/all_to_all | solution.py:172
  213.7 9.0 %all-to-all-done.3 = bf16[8,9,1664]{2,1,0:T(8,128)(2,1)S(1)} async-done(((bf16[8,9,1664]{2,1,0:T(8,128)(2,1)}), bf16[8,9,1664]{2,1,0:T(8,128)(2,1)S(1)}, u32[]{:S(2)}, u32[]{:S(2)}) %all-to-all-start.3) | async-done | bytes 239648 | tf_op jit(solution)/shard_map/all_to_all | solution.py:172
  223.4 0.9 multiply_convert_fusion
  225.1 58.3 %all-gather.11.cloned.1.call-done = bf16[2048,1664]{1,0:T(8,128)(2,1)} async-done(((bf16[128,1664]{1,0:T(8,128)(2,1)}), bf16[2048,1664]{1,0:T(8,128)(2,1)}) %all-gather.11.cloned.1.call-update) | async-done | bytes 6815760 | tf_op jit(solution)/shard_map/all_gather | solution.py:196
  283.3 5.7 %convolution_convert_fusion.1 = bf16[2048,312]{0,1:T(8,128)(2,1)S(1)} fusion(bf16[2048,1664]{1,0:T(8,128)(2,1)} %all-gather.11.cloned.1.call-done, bf16[1664,312]{0,1:T(8,128)(2,1)} %bitcast.190), kind=kOutput, calls=%fused_computation.37 | convolution fusion | flops 2127151104 | bytes 9132032 | tf_op jit(solution)/shard_map/dot_general | solution.py:29
  290.1 0.7 fusion.57
  291.9 1.0 fusion.56
  294.0 1.3 fusion.55
  296.0 0.8 fusion.27
  297.0 15.5 %all_to_all.40 = bf16[16,128,104]{1,2,0:T(8,128)(2,1)S(1)} all-to-all(bf16[16,128,104]{1,2,0:T(8,128)(2,1)S(1)} %copy.36), channel_id=1, replica_groups=mesh['seq'=16,'grp'=8] {'seq'}, dimensions={0} | all-to-all | bytes 851968 | tf_op jit(solution)/shard_map/all_to_all | solution.py:66
  312.5 1.9 convolution_add_fusion
  (88 shorter events, 11.1 us)
Async XLA Ops:
  6.5 156.0 %copy-start = (bf16[416,1664]{1,0:T(8,128)(2,1)S(1)}, bf16[416,1664]{1,0:T(8,128)(2,1)}, u32[]{:S(2)}) copy-start(bf16[416,1664]{1,0:T(8,128)(2,1)} %param.21) | copy-start | bytes 4153348
  6.5 70.8 %all-gather.5.cloned.1.call-start = ((), (), s32[]{:S(2)}) async-start(), calls=%async_computation.5 | async-start | bytes 7241728 | tf_op jit(solution)/shard_map/all_gather | solution.py:125
  11.2 127.3 %all-gather.7.cloned.1.call-start = ((), (), s32[]{:S(2)}) async-start(), calls=%async_computation.6 | async-start | bytes 5883904 | tf_op jit(solution)/shard_map/all_gather | solution.py:123
  11.9 212.4 %all-gather.9.cloned.1.call-start = ((), (), s32[]{:S(2)}) async-start(), calls=%async_computation.7 | async-start | bytes 5883904 | tf_op jit(solution)/shard_map/all_gather | solution.py:138
  100.1 38.4 %copy-start.1 = (bf16[128,1664]{1,0:T(8,128)(2,1)S(1)}, bf16[128,1664]{1,0:T(8,128)(2,1)}, u32[]{:S(2)}) copy-start(bf16[128,1664]{1,0:T(8,128)(2,1)} %param.16) | copy-start | bytes 1277956
  101.3 37.2 %all-to-all-start = ((bf16[16,128,104]{1,2,0:T(8,128)(2,1)}), bf16[16,128,104]{1,2,0:T(8,128)(2,1)S(1)}, u32[]{:S(2)}, u32[]{:S(2)}) async-start(bf16[16,128,104]{1,2,0:T(8,128)(2,1)} %copy_bitcast_fusion), calls=%async_computation | async-start | bytes 851968 | tf_op jit(solution)/shard_map/all_to_all | solution.py:66
  138.5 4.0 %copy-start.3 = (f32[1664]{0:T(1024)S(1)}, f32[1664]{0:T(1024)}, u32[]{:S(2)}) copy-start(f32[1664]{0:T(1024)} %param.20) | copy-start | bytes 19972
  164.9 3.9 %copy-start.7 = (s32[32,1]{0,1:T(1,128)S(1)}, s32[32,1]{0,1:T(1,128)}, u32[]{:S(2)}) copy-start(s32[32,1]{0,1:T(1,128)} %param.23) | copy-start | bytes 388
  164.9 58.0 %copy-start.2 = (bf16[128,1664]{1,0:T(8,128)(2,1)S(1)}, bf16[128,1664]{1,0:T(8,128)(2,1)}, u32[]{:S(2)}) copy-start(bf16[128,1664]{1,0:T(8,128)(2,1)} %param.26) | copy-start | bytes 1277956
  164.9 40.5 %all-to-all-start.2 = ((bf16[16,32,1664]{2,1,0:T(8,128)(2,1)}), bf16[16,32,1664]{2,1,0:T(8,128)(2,1)S(1)}, u32[]{:S(2)}, u32[]{:S(2)}) async-start(bf16[16,32,1664]{2,1,0:T(8,128)(2,1)} %bitcast.178), calls=%async_computation.2 | async-start | bytes 3407872 | tf_op jit(solution)/shard_map/all_to_all | solution.py:150
  168.7 54.7 %copy-start.4 = (f32[1664]{0:T(1024)S(1)}, f32[1664]{0:T(1024)}, u32[]{:S(2)}) copy-start(f32[1664]{0:T(1024)} %param.27) | copy-start | bytes 19972
  168.9 44.8 %copy-start.8 = (s32[1,1,128]{2,1,0:T(1,128)S(1)}, s32[1,1,128]{2,1,0:T(1,128)}, u32[]{:S(2)}) copy-start(s32[1,1,128]{2,1,0:T(1,128)} %param.24) | copy-start | bytes 1540
  209.0 13.7 %all-to-all-start.3 = ((bf16[8,9,1664]{2,1,0:T(8,128)(2,1)}), bf16[8,9,1664]{2,1,0:T(8,128)(2,1)S(1)}, u32[]{:S(2)}, u32[]{:S(2)}) async-start(bf16[8,9,1664]{2,1,0:T(8,128)(2,1)} %pad_maximum_fusion), calls=%async_computation.3 | async-start | bytes 851968 | tf_op jit(solution)/shard_map/all_to_all | solution.py:172
  213.5 69.9 %all-gather.11.cloned.1.call-start = ((), (), s32[]{:S(2)}) async-start(), calls=%async_computation.8 | async-start | bytes 7241728 | tf_op jit(solution)/shard_map/all_gather | solution.py:196
  225.0 64.0 %copy-start.5 = (pred[2048]{0:T(1024)(128)(4,1)}, pred[2048]{0:T(1024)(128)(4,1)S(1)}, u32[]{:S(2)}) copy-start(pred[2048]{0:T(1024)(128)(4,1)S(1)} %iota_compare_fusion.4) | copy-start | bytes 6148
  289.4 0.7 slice-start.2
  291.2 0.7 copy-start.6
  295.4 17.2 %slice-start = ((s8[5537792]{0:T(1024)(128)(4,1)}), s8[1343488]{0:T(1024)(128)(4,1)S(1)}, s32[]{:S(2)}) async-start(s8[5537792]{0:T(1024)(128)(4,1)} %bitcast.175), calls=%async_computation.9 | async-start | bytes 2686976
  296.0 16.5 %slice-start.1 = ((s8[5537792]{0:T(1024)(128)(4,1)}), s8[4194304]{0:T(1024)(128)(4,1)S(1)}, s32[]{:S(2)}) async-start(s8[5537792]{0:T(1024)(128)(4,1)} %bitcast.175), calls=%async_computation.10 | async-start | bytes 8388608
Sparse Core Ops, SparseCore 0:
  11.3 66.0 all-gather.4
  79.5 58.9 all-gather.6
  140.6 70.9 all-gather.8
  224.5 58.8 all-gather.10
where the time goes:
time: 322 us; the launch traced here: 321 us
  waiting for transfers between devices  199 us (62%)
  matrix products  34.8 us (11%)
  blocking collectives  34.5 us (11%)
  other arithmetic  18.8 us (6%)
  between operations  14.1 us (4%)
  starting transfers between devices  13.8 us (4%)
  local copies, waits for them, and re-layouts  6.3 us (2%)
    all_gather x1, waiting for transfers between devices, per_device(): lax.all_gather(vis_normed, 'seq', axis=0, tiled=True)  64.4 us
    all_gather x1, waiting for transfers between devices, per_device(): lax.all_gather(txt_normed, 'seq', axis=0, tiled=True)  58.3 us
    all_to_all x1, waiting for transfers between devices, per_device(): lax.all_to_all(merge_partial.astype(jnp.bfloat16).reshape(seq_count, -1,...  34.2 us
    all_gather x1, waiting for transfers between devices, per_device(): vis_out_full = lax.all_gather(vis_out, 'seq', axis=0, tiled=True)  31.9 us
    all_to_all x1, blocking collectives, per_device(): lax.all_to_all(merged_in, 'seq', split_axis=1, concat_axis=0, tiled=True)  19 us
    all_to_all x1, blocking collectives, heads_to_rows(): lax.all_to_all(blocks, 'seq', split_axis=0, concat_axis=0, tiled=True)  15.5 us
    dot_general x2, matrix products, projector(): jnp.dot(shard_piece, packed, preferred_element_type=jnp.float32)  11.3 us
    all_to_all x1, waiting for transfers between devices, per_device(): lax.all_to_all(jnp.concatenate([outgoing, flag_row], axis=1), 'grp', spli...  9.02 us
  transfers between devices with their start and end apart: 7, of which 5 were waited for; matrix products, arithmetic and copies ran while one was open for 12% of the time, Pallas kernels for 0%

commit v1 on v0

--- a/solution.py
+++ b/solution.py
@@ -4,6 +4,22 @@
 from jax.sharding import PartitionSpec as P
 
 HEAD_DIM = 104
+
+
+def collect(x, axis, dim):
+    ways, here, step = (lax.axis_size(axis), lax.axis_index(axis), x.shape[dim])
+    shape = [n * ways if d == dim else n for d, n in enumerate(x.shape)]
+    full = lax.dynamic_update_slice_in_dim(jnp.zeros(shape, x.dtype), x, here * step, axis=dim)
+    going_up = going_down = x
+    for far in range(1, ways // 2 + 1):
+        going_up = lax.ppermute(going_up, axis, [(d, (d + 1) % ways) for d in range(ways)])
+        full = lax.dynamic_update_slice_in_dim(full, going_up, (here - far) % ways * step, axis=dim)
+        if 2 * far < ways:
+            going_down = lax.ppermute(going_down, axis, [(d, (d - 1) % ways) for d in range(ways)])
+            full = lax.dynamic_update_slice_in_dim(
+                full, going_down, (here + far) % ways * step, axis=dim
+            )
+    return full
 
 
 def layer_norm(row_block, scale_gain):
@@ -122,7 +138,7 @@
     group_patches = token_count * seq_count
     vis_out_full = lax.all_gather(vis_out, "seq", axis=0, tiled=True)
     vis_normed = layer_norm(patches, vis_gain).astype(jnp.bfloat16)
-    vis_proj = projector(vis_qkv, lax.all_gather(vis_normed, "seq", axis=0, tiled=True))
+    vis_proj = projector(vis_qkv, collect(vis_normed, "seq", 0))
     bounds = jnp.cumsum(image_blocks[0])[:-1]
 
     def segment(indices):

time: 322 us -> 359 us (1.11)
  starting transfers between devices: 13.8 us -> 47.2 us
  waiting for transfers between devices: 199 us -> 183 us
  local copies, waits for them, and re-layouts: 6.3 us -> 21.2 us
  blocking collectives: 34.5 us -> 40.7 us
  other arithmetic: 18.8 us -> 14.6 us
    ppermute x0 -> x15, waiting for transfers between devices: none -> 77.1 us  [the longest x8 66.4 us: collect(): lax.ppermute(going_up, axis, [(d, (d + 1) % ways) for d in range(ways)])]
    all_gather x1 -> x0, waiting for transfers between devices: 64.4 us -> none  [per_device(): lax.all_gather(vis_normed, 'seq', axis=0, tiled=True)]
    ppermute x0 -> x15, starting transfers between devices: none -> 38.8 us  [the longest x7 37.2 us: collect(): lax.ppermute(going_down, axis, [(d, (d - 1) % ways) for d in range(ways)])]
    all_gather x1, waiting for transfers between devices: 31.9 us -> 0.01 us  [per_device(): vis_out_full = lax.all_gather(vis_out, 'seq', axis=0, tiled=True)]
    all_to_all x1 -> x2, blocking collectives: 15.5 us -> 27.6 us  [heads_to_rows(): lax.all_to_all(blocks, 'seq', split_axis=0, concat_axis=0, tiled=True)]
    dynamic_update_slice x0 -> x15, local copies, waits for them, and re-layouts: none -> 11.9 us  [the longest x8 6.37 us: collect(): lax.dynamic_update_slice_in_dim(full, going_up, (here - far) % ways * ste...]
    all_to_all x1, blocking collectives: 19 us -> 13 us  [per_device(): lax.all_to_all(merged_in, 'seq', split_axis=1, concat_axis=0, tiled=True)]
    all_to_all x1 -> x0, starting transfers between devices: 5.26 us -> none  [heads_to_rows(): lax.all_to_all(blocks, 'seq', split_axis=0, concat_axis=0, tiled=True)]
  transfers between devices with their start and end apart: 7 -> 20, of which waited for: 5 -> 14; matrix products, arithmetic and copies ran while one was open for 12% -> 14% of each run, Pallas kernels for 0% -> 0%
where the time goes in v1:
time: 359 us; the launch traced here: 358 us
  waiting for transfers between devices  183 us (51%)
  starting transfers between devices  47.2 us (13%)
  blocking collectives  40.7 us (11%)
  matrix products  37.3 us (10%)
  local copies, waits for them, and re-layouts  21.2 us (6%)
  other arithmetic  14.6 us (4%)
  between operations  14.4 us (4%)
    ppermute x8, waiting for transfers between devices, collect(): lax.ppermute(going_up, axis, [(d, (d + 1) % ways) for d in range(ways)])  66.4 us
    all_gather x1, waiting for transfers between devices, per_device(): lax.all_gather(txt_normed, 'seq', axis=0, tiled=True)  58.5 us
    all_to_all x1, waiting for transfers between devices, per_device(): lax.all_to_all(merge_partial.astype(jnp.bfloat16).reshape(seq_count, -1,...  38.2 us
    ppermute x7, starting transfers between devices, collect(): lax.ppermute(going_down, axis, [(d, (d - 1) % ways) for d in range(ways)])  37.2 us
    all_to_all x2, blocking collectives, heads_to_rows(): lax.all_to_all(blocks, 'seq', split_axis=0, concat_axis=0, tiled=True)  27.6 us
    all_to_all x1, blocking collectives, per_device(): lax.all_to_all(merged_in, 'seq', split_axis=1, concat_axis=0, tiled=True)  13 us
    dot_general x2, matrix products, projector(): jnp.dot(shard_piece, packed, preferred_element_type=jnp.float32)  11.1 us
    ppermute x7, waiting for transfers between devices, collect(): lax.ppermute(going_down, axis, [(d, (d - 1) % ways) for d in range(ways)])  10.6 us
  transfers between devices with their start and end apart: 20, of which 14 were waited for; matrix products, arithmetic and copies ran while one was open for 14% of the time, Pallas kernels for 0%

profile of v1, /device:TPU:0, one launch (start us, length us, event | category | flops | bytes accessed | tf_op | source)
XLA Modules:
  0.0 358.0 jit_solution(9299421530355107676)
XLA Ops:
  6.6 1.3 convert_reduce_fusion.1
  7.8 1.3 fusion.35
  9.1 3.3 broadcast_in_dim.37
  12.4 1.1 constant_dynamic-update-slice_fusion.15
  13.5 1.6 collective-permute-start
  15.1 3.7 %collective-permute-start.1 = (bf16[128,1664]{1,0:T(8,128)(2,1)S(1)}, bf16[128,1664]{1,0:T(8,128)(2,1)S(1)}, u32[]{:S(2)}, u32[]{:S(2)}) collective-permute-start(bf16[128,1664]{1,0:T(8,128)(2,1)S(1)} %get-tuple-element.149), channel_id=1, source_target_pairs={{0,120},{8,0},{16,8},{24,16},{32,24},{40,32},{48,40},{56,48},{64,5... | collective-permute-start | bytes 1277960 | tf_op jit(solution)/shard_map/ppermute | solution.py:18
  19.4 9.2 %collective-permute-done = bf16[128,1664]{1,0:T(8,128)(2,1)S(1)} collective-permute-done((bf16[128,1664]{1,0:T(8,128)(2,1)S(1)}, bf16[128,1664]{1,0:T(8,128)(2,1)S(1)}, u32[]{:S(2)}, u32[]{:S(2)}) %collective-permute-start) | collective-permute-done | bytes 426016 | tf_op jit(solution)/shard_map/ppermute | solution.py:15
  28.6 5.3 %collective-permute-start.3 = (bf16[128,1664]{1,0:T(8,128)(2,1)S(1)}, bf16[128,1664]{1,0:T(8,128)(2,1)S(1)}, u32[]{:S(2)}, u32[]{:S(2)}) collective-permute-start(bf16[128,1664]{1,0:T(8,128)(2,1)S(1)} %collective-permute-done.1), channel_id=1, source_target_pairs={{0,120},{8,0},{16,8},{24,16},{32,24},{40,32},{48,40},{56,48},{64,5... | collective-permute-start | bytes 1277960 | tf_op jit(solution)/shard_map/ppermute | solution.py:18
  35.5 12.9 %collective-permute-done.2 = bf16[128,1664]{1,0:T(8,128)(2,1)S(1)} collective-permute-done((bf16[128,1664]{1,0:T(8,128)(2,1)S(1)}, bf16[128,1664]{1,0:T(8,128)(2,1)S(1)}, u32[]{:S(2)}, u32[]{:S(2)}) %collective-permute-start.2) | collective-permute-done | bytes 426016 | tf_op jit(solution)/shard_map/ppermute | solution.py:15
  48.5 5.3 %collective-permute-start.5 = (bf16[128,1664]{1,0:T(8,128)(2,1)S(1)}, bf16[128,1664]{1,0:T(8,128)(2,1)S(1)}, u32[]{:S(2)}, u32[]{:S(2)}) collective-permute-start(bf16[128,1664]{1,0:T(8,128)(2,1)S(1)} %collective-permute-done.3), channel_id=1, source_target_pairs={{0,120},{8,0},{16,8},{24,16},{32,24},{40,32},{48,40},{56,48},{64,5... | collective-permute-start | bytes 1277960 | tf_op jit(solution)/shard_map/ppermute | solution.py:18
  55.4 9.2 %collective-permute-done.4 = bf16[128,1664]{1,0:T(8,128)(2,1)S(1)} collective-permute-done((bf16[128,1664]{1,0:T(8,128)(2,1)S(1)}, bf16[128,1664]{1,0:T(8,128)(2,1)S(1)}, u32[]{:S(2)}, u32[]{:S(2)}) %collective-permute-start.4) | collective-permute-done | bytes 426016 | tf_op jit(solution)/shard_map/ppermute | solution.py:15
  64.6 5.1 %collective-permute-done.5 = bf16[128,1664]{1,0:T(8,128)(2,1)S(1)} collective-permute-done((bf16[128,1664]{1,0:T(8,128)(2,1)S(1)}, bf16[128,1664]{1,0:T(8,128)(2,1)S(1)}, u32[]{:S(2)}, u32[]{:S(2)}) %collective-permute-start.5) | collective-permute-done | bytes 426016 | tf_op jit(solution)/shard_map/ppermute | solution.py:18
  69.7 5.8 %collective-permute-start.7 = (bf16[128,1664]{1,0:T(8,128)(2,1)S(1)}, bf16[128,1664]{1,0:T(8,128)(2,1)S(1)}, u32[]{:S(2)}, u32[]{:S(2)}) collective-permute-start(bf16[128,1664]{1,0:T(8,128)(2,1)S(1)} %collective-permute-done.5), channel_id=1, source_target_pairs={{0,120},{8,0},{16,8},{24,16},{32,24},{40,32},{48,40},{56,48},{64,5... | collective-permute-start | bytes 1277960 | tf_op jit(solution)/shard_map/ppermute | solution.py:18
  77.1 11.2 %collective-permute-done.6 = bf16[128,1664]{1,0:T(8,128)(2,1)S(1)} collective-permute-done((bf16[128,1664]{1,0:T(8,128)(2,1)S(1)}, bf16[128,1664]{1,0:T(8,128)(2,1)S(1)}, u32[]{:S(2)}, u32[]{:S(2)}) %collective-permute-start.6) | collective-permute-done | bytes 426016 | tf_op jit(solution)/shard_map/ppermute | solution.py:15
  88.3 4.5 %collective-permute-done.7 = bf16[128,1664]{1,0:T(8,128)(2,1)S(1)} collective-permute-done((bf16[128,1664]{1,0:T(8,128)(2,1)S(1)}, bf16[128,1664]{1,0:T(8,128)(2,1)S(1)}, u32[]{:S(2)}, u32[]{:S(2)}) %collective-permute-start.7) | collective-permute-done | bytes 426016 | tf_op jit(solution)/shard_map/ppermute | solution.py:18
  92.8 5.8 %collective-permute-start.9 = (bf16[128,1664]{1,0:T(8,128)(2,1)S(1)}, bf16[128,1664]{1,0:T(8,128)(2,1)S(1)}, u32[]{:S(2)}, u32[]{:S(2)}) collective-permute-start(bf16[128,1664]{1,0:T(8,128)(2,1)S(1)} %collective-permute-done.7), channel_id=1, source_target_pairs={{0,120},{8,0},{16,8},{24,16},{32,24},{40,32},{48,40},{56,48},{64,5... | collective-permute-start | bytes 1277960 | tf_op jit(solution)/shard_map/ppermute | solution.py:18
  100.2 3.0 collective-permute-done.8
  103.3 1.0 collective-permute-done.9
  104.3 5.8 %collective-permute-start.11 = (bf16[128,1664]{1,0:T(8,128)(2,1)S(1)}, bf16[128,1664]{1,0:T(8,128)(2,1)S(1)}, u32[]{:S(2)}, u32[]{:S(2)}) collective-permute-start(bf16[128,1664]{1,0:T(8,128)(2,1)S(1)} %collective-permute-done.9), channel_id=1, source_target_pairs={{0,120},{8,0},{16,8},{24,16},{32,24},{40,32},{48,40},{56,48},{64,5... | collective-permute-start | bytes 1277960 | tf_op jit(solution)/shard_map/ppermute | solution.py:18
  111.7 5.1 %collective-permute-done.10 = bf16[128,1664]{1,0:T(8,128)(2,1)S(1)} collective-permute-done((bf16[128,1664]{1,0:T(8,128)(2,1)S(1)}, bf16[128,1664]{1,0:T(8,128)(2,1)S(1)}, u32[]{:S(2)}, u32[]{:S(2)}) %collective-permute-start.10) | collective-permute-done | bytes 426016 | tf_op jit(solution)/shard_map/ppermute | solution.py:15
  116.7 5.3 %collective-permute-start.13 = (bf16[128,1664]{1,0:T(8,128)(2,1)S(1)}, bf16[128,1664]{1,0:T(8,128)(2,1)S(1)}, u32[]{:S(2)}, u32[]{:S(2)}) collective-permute-start(bf16[128,1664]{1,0:T(8,128)(2,1)S(1)} %collective-permute-done.11), channel_id=1, source_target_pairs={{0,120},{8,0},{16,8},{24,16},{32,24},{40,32},{48,40},{56,48},{64,5... | collective-permute-start | bytes 1277960 | tf_op jit(solution)/shard_map/ppermute | solution.py:18
  123.6 5.7 %collective-permute-done.12 = bf16[128,1664]{1,0:T(8,128)(2,1)S(1)} collective-permute-done((bf16[128,1664]{1,0:T(8,128)(2,1)S(1)}, bf16[128,1664]{1,0:T(8,128)(2,1)S(1)}, u32[]{:S(2)}, u32[]{:S(2)}) %collective-permute-start.12) | collective-permute-done | bytes 426016 | tf_op jit(solution)/shard_map/ppermute | solution.py:15
  131.0 10.2 %collective-permute-done.14 = bf16[128,1664]{1,0:T(8,128)(2,1)S(1)} collective-permute-done((bf16[128,1664]{1,0:T(8,128)(2,1)S(1)}, bf16[128,1664]{1,0:T(8,128)(2,1)S(1)}, u32[]{:S(2)}, u32[]{:S(2)}) %collective-permute-start.14) | collective-permute-done | bytes 426016 | tf_op jit(solution)/shard_map/ppermute | solution.py:15
  141.9 5.5 %convolution_convert_fusion.2 = bf16[2048,312]{0,1:T(8,128)(2,1)S(1)} fusion(bf16[2048,1664]{1,0:T(8,128)(2,1)} %constant_dynamic-update-slice_fusion, bf16[1664,312]{0,1:T(8,128)(2,1)S(1)} %bitcast.189), kind=kOutput, calls=%fused_computation.38 | convolution fusion | flops 2127151104 | bytes 9132032 | tf_op jit(solution)/shard_map/dot_general | solution.py:45
  147.9 19.5 %while.12 = (s32[]{:T(128)}, bf16[4,512,1,104]{1,3,2,0:T(8,128)(2,1)}, s32[4]{0:T(128)S(1)}, s32[3]{0:T(128)S(1)}, s32[2048]{0:T(1024)S(1)}, /*index=5*/bf16[4,5...) while((s32[]{:T(128)}, ...), condition=%wide.region_10.11_spmd, body=%wide.region_6.10_spmd.sunk | while | flops 445709312 | bytes 13675133 | solution.py:74
  151.0 1.7 fusion.78
  154.2 1.0 fusion.76
  155.9 1.7 fusion.78
  159.0 1.0 fusion.76
  160.7 1.7 fusion.78
  163.9 1.0 fusion.76
  165.6 1.7 fusion.78
  167.3 1.2 copy.29
  168.7 12.2 %all_to_all.39 = bf16[16,128,104]{1,2,0:T(8,128)(2,1)S(1)} all-to-all(bf16[16,128,104]{1,2,0:T(8,128)(2,1)S(1)} %copy_bitcast_fusion), channel_id=1, replica_groups=mesh['seq'=16,'grp'=8] {'seq'}, dimensions={0} | all-to-all | bytes 851968 | tf_op jit(solution)/shard_map/all_to_all | solution.py:82
  180.9 3.8 %fusion.55 = (f32[128]{0:T(128)S(1)}, f32[128,1664]{1,0:T(8,128)S(1)}) fusion(bf16[128,1664]{0,1:T(8,128)(2,1)S(1)} %bitcast.177, bf16[1664,1664]{1,0:T(8,128)(2,1)} %all-gather.4.cloned.1.call-done, bf16[128,1664]{1,0:T(8,128)(2,1)S(1)} %copy-done.1), kind=kOutput, calls=%fused_computation.155 | convolution fusion | flops 709476224 | bytes 7242240 | tf_op jit(solution)/shard_map/dot_general | solution.py:155
  186.1 13.0 %all_to_all.40 = bf16[32,16,416]{2,0,1:T(8,128)(2,1)S(1)} all-to-all(bf16[32,16,416]{2,0,1:T(8,128)(2,1)S(1)} %copy.31), channel_id=1, replica_groups=mesh['seq'=16,'grp'=8] {'seq'}, dimensions={1} | all-to-all | bytes 851968 | tf_op jit(solution)/shard_map/all_to_all | solution.py:164
  199.1 2.3 convolution_convert_fusion
  201.4 3.8 %all-to-all-start.2 = ((bf16[16,32,1664]{2,1,0:T(8,128)(2,1)}), bf16[16,32,1664]{2,1,0:T(8,128)(2,1)S(1)}, u32[]{:S(2)}, u32[]{:S(2)}) async-start(bf16[16,32,1664]{2,1,0:T(8,128)(2,1)} %bitcast.178), calls=%async_computation.2 | async-start | bytes 3407872 | tf_op jit(solution)/shard_map/all_to_all | solution.py:166
  205.8 38.2 %all-to-all-done.2 = bf16[16,32,1664]{2,1,0:T(8,128)(2,1)S(1)} async-done(((bf16[16,32,1664]{2,1,0:T(8,128)(2,1)}), bf16[16,32,1664]{2,1,0:T(8,128)(2,1)S(1)}, u32[]{:S(2)}, u32[]{:S(2)}) %all-to-all-start.2) | async-done | bytes 1703968 | tf_op jit(solution)/shard_map/all_to_all | solution.py:166
  245.2 4.2 %all-to-all-start.3 = ((bf16[8,9,1664]{2,1,0:T(8,128)(2,1)}), bf16[8,9,1664]{2,1,0:T(8,128)(2,1)S(1)}, u32[]{:S(2)}, u32[]{:S(2)}) async-start(bf16[8,9,1664]{2,1,0:T(8,128)(2,1)} %pad_maximum_fusion), calls=%async_computation.3 | async-start | bytes 851968 | tf_op jit(solution)/shard_map/all_to_all | solution.py:188
  249.7 9.0 %all-to-all-done.3 = bf16[8,9,1664]{2,1,0:T(8,128)(2,1)S(1)} async-done(((bf16[8,9,1664]{2,1,0:T(8,128)(2,1)}), bf16[8,9,1664]{2,1,0:T(8,128)(2,1)S(1)}, u32[]{:S(2)}, u32[]{:S(2)}) %all-to-all-start.3) | async-done | bytes 239648 | tf_op jit(solution)/shard_map/all_to_all | solution.py:188
  258.9 1.5 multiply_reduce_fusion
  262.1 58.5 %all-gather.8.cloned.1.call-done = bf16[2048,1664]{1,0:T(8,128)(2,1)} async-done(((bf16[128,1664]{1,0:T(8,128)(2,1)}), bf16[2048,1664]{1,0:T(8,128)(2,1)}) %all-gather.8.cloned.1.call-update) | async-done | bytes 6815760 | tf_op jit(solution)/shard_map/all_gather | solution.py:212
  320.6 5.7 %convolution_convert_fusion.1 = bf16[2048,312]{0,1:T(8,128)(2,1)S(1)} fusion(bf16[2048,1664]{1,0:T(8,128)(2,1)} %all-gather.8.cloned.1.call-done, bf16[1664,312]{0,1:T(8,128)(2,1)} %bitcast.190), kind=kOutput, calls=%fused_computation.37 | convolution fusion | flops 2127151104 | bytes 9132032 | tf_op jit(solution)/shard_map/dot_general | solution.py:45
  328.9 1.0 fusion.57
  331.1 1.3 fusion.56
  334.1 15.5 %all_to_all.41 = bf16[16,128,104]{1,2,0:T(8,128)(2,1)S(1)} all-to-all(bf16[16,128,104]{1,2,0:T(8,128)(2,1)S(1)} %copy.36), channel_id=1, replica_groups=mesh['seq'=16,'grp'=8] {'seq'}, dimensions={0} | all-to-all | bytes 851968 | tf_op jit(solution)/shard_map/all_to_all | solution.py:82
  349.6 1.9 convolution_add_fusion
  (134 shorter events, 32.5 us)
Async XLA Ops:
  6.5 192.6 %copy-start = (bf16[416,1664]{1,0:T(8,128)(2,1)S(1)}, bf16[416,1664]{1,0:T(8,128)(2,1)}, u32[]{:S(2)}) copy-start(bf16[416,1664]{1,0:T(8,128)(2,1)} %param.21) | copy-start | bytes 4153348
  6.5 5.9 %copy-start.1 = (bf16[128,1664]{1,0:T(8,128)(2,1)S(1)}, bf16[128,1664]{1,0:T(8,128)(2,1)}, u32[]{:S(2)}) copy-start(bf16[128,1664]{1,0:T(8,128)(2,1)} %param.16) | copy-start | bytes 1277956
  6.5 5.9 %copy-start.2 = (f32[1664]{0:T(1024)S(1)}, f32[1664]{0:T(1024)}, u32[]{:S(2)}) copy-start(f32[1664]{0:T(1024)} %param.17) | copy-start | bytes 19972
  6.5 174.4 %all-gather.4.cloned.1.call-start = ((), (), s32[]{:S(2)}) async-start(), calls=%async_computation.5 | async-start | bytes 5883904 | tf_op jit(solution)/shard_map/all_gather | solution.py:139
  9.1 10.0 %copy-start.9 = (s32[1,4]{1,0:T(1,128)S(1)}, s32[1,4]{1,0:T(1,128)}, u32[]{:S(2)}) copy-start(s32[1,4]{1,0:T(1,128)} %param.22) | copy-start | bytes 52
  13.5 15.1 %collective-permute-start = (bf16[128,1664]{1,0:T(8,128)(2,1)S(1)}, bf16[128,1664]{1,0:T(8,128)(2,1)S(1)}, u32[]{:S(2)}, u32[]{:S(2)}) collective-permute-start(bf16[128,1664]{1,0:T(8,128)(2,1)S(1)} %get-tuple-element.149), channel_id=1, source_target_pairs={{0,8},{8,16},{16,24},{24,32},{32,40},{40,48},{48,56},{56,64},{64,7... | collective-permute-start | bytes 1277960 | tf_op jit(solution)/shard_map/ppermute | solution.py:15
  15.1 13.5 %collective-permute-start.1 = (bf16[128,1664]{1,0:T(8,128)(2,1)S(1)}, bf16[128,1664]{1,0:T(8,128)(2,1)S(1)}, u32[]{:S(2)}, u32[]{:S(2)}) collective-permute-start(bf16[128,1664]{1,0:T(8,128)(2,1)S(1)} %get-tuple-element.149), channel_id=1, source_target_pairs={{0,120},{8,0},{16,8},{24,16},{32,24},{40,32},{48,40},{56,48},{64,5... | collective-permute-start | bytes 1277960 | tf_op jit(solution)/shard_map/ppermute | solution.py:18
  18.8 242.5 %all-gather.6.cloned.1.call-start = ((), (), s32[]{:S(2)}) async-start(), calls=%async_computation.6 | async-start | bytes 5883904 | tf_op jit(solution)/shard_map/all_gather | solution.py:154
  28.6 19.8 %collective-permute-start.2 = (bf16[128,1664]{1,0:T(8,128)(2,1)S(1)}, bf16[128,1664]{1,0:T(8,128)(2,1)S(1)}, u32[]{:S(2)}, u32[]{:S(2)}) collective-permute-start(bf16[128,1664]{1,0:T(8,128)(2,1)S(1)} %collective-permute-done), channel_id=1, source_target_pairs={{0,8},{8,16},{16,24},{24,32},{32,40},{40,48},{48,56},{56,64},{64,7... | collective-permute-start | bytes 1277960 | tf_op jit(solution)/shard_map/ppermute | solution.py:15
  28.6 19.8 %collective-permute-start.3 = (bf16[128,1664]{1,0:T(8,128)(2,1)S(1)}, bf16[128,1664]{1,0:T(8,128)(2,1)S(1)}, u32[]{:S(2)}, u32[]{:S(2)}) collective-permute-start(bf16[128,1664]{1,0:T(8,128)(2,1)S(1)} %collective-permute-done.1), channel_id=1, source_target_pairs={{0,120},{8,0},{16,8},{24,16},{32,24},{40,32},{48,40},{56,48},{64,5... | collective-permute-start | bytes 1277960 | tf_op jit(solution)/shard_map/ppermute | solution.py:18
  48.4 16.2 %collective-permute-start.4 = (bf16[128,1664]{1,0:T(8,128)(2,1)S(1)}, bf16[128,1664]{1,0:T(8,128)(2,1)S(1)}, u32[]{:S(2)}, u32[]{:S(2)}) collective-permute-start(bf16[128,1664]{1,0:T(8,128)(2,1)S(1)} %collective-permute-done.2), channel_id=1, source_target_pairs={{0,8},{8,16},{16,24},{24,32},{32,40},{40,48},{48,56},{56,64},{64,7... | collective-permute-start | bytes 1277960 | tf_op jit(solution)/shard_map/ppermute | solution.py:15
  48.5 21.2 %collective-permute-start.5 = (bf16[128,1664]{1,0:T(8,128)(2,1)S(1)}, bf16[128,1664]{1,0:T(8,128)(2,1)S(1)}, u32[]{:S(2)}, u32[]{:S(2)}) collective-permute-start(bf16[128,1664]{1,0:T(8,128)(2,1)S(1)} %collective-permute-done.3), channel_id=1, source_target_pairs={{0,120},{8,0},{16,8},{24,16},{32,24},{40,32},{48,40},{56,48},{64,5... | collective-permute-start | bytes 1277960 | tf_op jit(solution)/shard_map/ppermute | solution.py:18
  64.6 23.7 %collective-permute-start.6 = (bf16[128,1664]{1,0:T(8,128)(2,1)S(1)}, bf16[128,1664]{1,0:T(8,128)(2,1)S(1)}, u32[]{:S(2)}, u32[]{:S(2)}) collective-permute-start(bf16[128,1664]{1,0:T(8,128)(2,1)S(1)} %collective-permute-done.4), channel_id=1, source_target_pairs={{0,8},{8,16},{16,24},{24,32},{32,40},{40,48},{48,56},{56,64},{64,7... | collective-permute-start | bytes 1277960 | tf_op jit(solution)/shard_map/ppermute | solution.py:15
  69.7 23.1 %collective-permute-start.7 = (bf16[128,1664]{1,0:T(8,128)(2,1)S(1)}, bf16[128,1664]{1,0:T(8,128)(2,1)S(1)}, u32[]{:S(2)}, u32[]{:S(2)}) collective-permute-start(bf16[128,1664]{1,0:T(8,128)(2,1)S(1)} %collective-permute-done.5), channel_id=1, source_target_pairs={{0,120},{8,0},{16,8},{24,16},{32,24},{40,32},{48,40},{56,48},{64,5... | collective-permute-start | bytes 1277960 | tf_op jit(solution)/shard_map/ppermute | solution.py:18
  76.3 65.6 %copy-start.8 = (bf16[3,1664,104]{1,2,0:T(8,128)(2,1)S(1)}, bf16[3,1664,104]{1,2,0:T(8,128)(2,1)}, u32[]{:S(2)}) copy-start(bf16[3,1664,104]{1,2,0:T(8,128)(2,1)} %param.18) | copy-start | bytes 3115012
  88.3 14.9 %collective-permute-start.8 = (bf16[128,1664]{1,0:T(8,128)(2,1)S(1)}, bf16[128,1664]{1,0:T(8,128)(2,1)S(1)}, u32[]{:S(2)}, u32[]{:S(2)}) collective-permute-start(bf16[128,1664]{1,0:T(8,128)(2,1)S(1)} %collective-permute-done.6), channel_id=1, source_target_pairs={{0,8},{8,16},{16,24},{24,32},{32,40},{40,48},{48,56},{56,64},{64,7... | collective-permute-start | bytes 1277960 | tf_op jit(solution)/shard_map/ppermute | solution.py:15
  92.8 11.4 %collective-permute-start.9 = (bf16[128,1664]{1,0:T(8,128)(2,1)S(1)}, bf16[128,1664]{1,0:T(8,128)(2,1)S(1)}, u32[]{:S(2)}, u32[]{:S(2)}) collective-permute-start(bf16[128,1664]{1,0:T(8,128)(2,1)S(1)} %collective-permute-done.7), channel_id=1, source_target_pairs={{0,120},{8,0},{16,8},{24,16},{32,24},{40,32},{48,40},{56,48},{64,5... | collective-permute-start | bytes 1277960 | tf_op jit(solution)/shard_map/ppermute | solution.py:18
  103.2 13.5 %collective-permute-start.10 = (bf16[128,1664]{1,0:T(8,128)(2,1)S(1)}, bf16[128,1664]{1,0:T(8,128)(2,1)S(1)}, u32[]{:S(2)}, u32[]{:S(2)}) collective-permute-start(bf16[128,1664]{1,0:T(8,128)(2,1)S(1)} %collective-permute-done.8), channel_id=1, source_target_pairs={{0,8},{8,16},{16,24},{24,32},{32,40},{40,48},{48,56},{56,64},{64,7... | collective-permute-start | bytes 1277960 | tf_op jit(solution)/shard_map/ppermute | solution.py:15
  104.3 12.5 %collective-permute-start.11 = (bf16[128,1664]{1,0:T(8,128)(2,1)S(1)}, bf16[128,1664]{1,0:T(8,128)(2,1)S(1)}, u32[]{:S(2)}, u32[]{:S(2)}) collective-permute-start(bf16[128,1664]{1,0:T(8,128)(2,1)S(1)} %collective-permute-done.9), channel_id=1, source_target_pairs={{0,120},{8,0},{16,8},{24,16},{32,24},{40,32},{48,40},{56,48},{64,5... | collective-permute-start | bytes 1277960 | tf_op jit(solution)/shard_map/ppermute | solution.py:18
  116.7 12.6 %collective-permute-start.12 = (bf16[128,1664]{1,0:T(8,128)(2,1)S(1)}, bf16[128,1664]{1,0:T(8,128)(2,1)S(1)}, u32[]{:S(2)}, u32[]{:S(2)}) collective-permute-start(bf16[128,1664]{1,0:T(8,128)(2,1)S(1)} %collective-permute-done.10), channel_id=1, source_target_pairs={{0,8},{8,16},{16,24},{24,32},{32,40},{40,48},{48,56},{56,64},{64,7... | collective-permute-start | bytes 1277960 | tf_op jit(solution)/shard_map/ppermute | solution.py:15
  116.7 13.4 %collective-permute-start.13 = (bf16[128,1664]{1,0:T(8,128)(2,1)S(1)}, bf16[128,1664]{1,0:T(8,128)(2,1)S(1)}, u32[]{:S(2)}, u32[]{:S(2)}) collective-permute-start(bf16[128,1664]{1,0:T(8,128)(2,1)S(1)} %collective-permute-done.11), channel_id=1, source_target_pairs={{0,120},{8,0},{16,8},{24,16},{32,24},{40,32},{48,40},{56,48},{64,5... | collective-permute-start | bytes 1277960 | tf_op jit(solution)/shard_map/ppermute | solution.py:18
  129.3 11.8 %collective-permute-start.14 = (bf16[128,1664]{1,0:T(8,128)(2,1)S(1)}, bf16[128,1664]{1,0:T(8,128)(2,1)S(1)}, u32[]{:S(2)}, u32[]{:S(2)}) collective-permute-start(bf16[128,1664]{1,0:T(8,128)(2,1)S(1)} %collective-permute-done.12), channel_id=1, source_target_pairs={{0,8},{8,16},{16,24},{24,32},{32,40},{40,48},{48,56},{56,64},{64,7... | collective-permute-start | bytes 1277960 | tf_op jit(solution)/shard_map/ppermute | solution.py:15
  180.9 4.0 %copy-start.3 = (f32[1664]{0:T(1024)S(1)}, f32[1664]{0:T(1024)}, u32[]{:S(2)}) copy-start(f32[1664]{0:T(1024)} %param.20) | copy-start | bytes 19972
  199.1 6.2 %copy-start.7 = (s32[32,1]{0,1:T(1,128)S(1)}, s32[32,1]{0,1:T(1,128)}, u32[]{:S(2)}) copy-start(s32[32,1]{0,1:T(1,128)} %param.23) | copy-start | bytes 388
  201.4 48.3 %copy-start.10 = (s32[1,1,128]{2,1,0:T(1,128)S(1)}, s32[1,1,128]{2,1,0:T(1,128)}, u32[]{:S(2)}) copy-start(s32[1,1,128]{2,1,0:T(1,128)} %param.24) | copy-start | bytes 1540
  201.4 59.0 %copy-start.4 = (f32[1664]{0:T(1024)S(1)}, f32[1664]{0:T(1024)}, u32[]{:S(2)}) copy-start(f32[1664]{0:T(1024)} %param.27) | copy-start | bytes 19972
  201.4 42.5 %all-to-all-start.2 = ((bf16[16,32,1664]{2,1,0:T(8,128)(2,1)}), bf16[16,32,1664]{2,1,0:T(8,128)(2,1)S(1)}, u32[]{:S(2)}, u32[]{:S(2)}) async-start(bf16[16,32,1664]{2,1,0:T(8,128)(2,1)} %bitcast.178), calls=%async_computation.2 | async-start | bytes 3407872 | tf_op jit(solution)/shard_map/all_to_all | solution.py:166
  245.2 13.5 %all-to-all-start.3 = ((bf16[8,9,1664]{2,1,0:T(8,128)(2,1)}), bf16[8,9,1664]{2,1,0:T(8,128)(2,1)S(1)}, u32[]{:S(2)}, u32[]{:S(2)}) async-start(bf16[8,9,1664]{2,1,0:T(8,128)(2,1)} %pad_maximum_fusion), calls=%async_computation.3 | async-start | bytes 851968 | tf_op jit(solution)/shard_map/all_to_all | solution.py:188
  249.5 71.1 %all-gather.8.cloned.1.call-start = ((), (), s32[]{:S(2)}) async-start(), calls=%async_computation.7 | async-start | bytes 7241728 | tf_op jit(solution)/shard_map/all_gather | solution.py:212
  262.0 64.2 %copy-start.5 = (pred[2048]{0:T(1024)(128)(4,1)}, pred[2048]{0:T(1024)(128)(4,1)S(1)}, u32[]{:S(2)}) copy-start(pred[2048]{0:T(1024)(128)(4,1)S(1)} %iota_compare_fusion.4) | copy-start | bytes 6148
  326.2 0.9 slice-start.2
  328.3 0.7 copy-start.6
  332.4 17.1 %slice-start = ((s8[5537792]{0:T(1024)(128)(4,1)}), s8[1343488]{0:T(1024)(128)(4,1)S(1)}, s32[]{:S(2)}) async-start(s8[5537792]{0:T(1024)(128)(4,1)} %bitcast.175), calls=%async_computation.8 | async-start | bytes 2686976
  333.1 16.5 %slice-start.1 = ((s8[5537792]{0:T(1024)(128)(4,1)}), s8[4194304]{0:T(1024)(128)(4,1)S(1)}, s32[]{:S(2)}) async-start(s8[5537792]{0:T(1024)(128)(4,1)} %bitcast.175), calls=%async_computation.9 | async-start | bytes 8388608
Sparse Core Ops, SparseCore 0:
  19.0 79.1 all-gather.3
  168.8 73.1 all-gather.5
  261.5 59.0 all-gather.7
